TPU v7x, 128 devices: a whole 4x4x4 slice. The times are simulated.
128 devices in a mesh: dp: 16 (over z, y), vocab: 8 (over x, core).
Axes of the slice: x: 4, y: 4, z: 4, core: 2. Of those that a mesh axis runs over, the one named last changes fastest.
Arguments:
- hidden: bfloat16 [32, 512, 1024], P('dp'), may hold values from -24 to 24
- norm_gain: float32 [1024], replicated, may hold values from 0.5 to 1.5
- head: bfloat16 [1024, 32000], P('dp', 'vocab'), may hold values from -4 to 4
- targets: int32 [32, 512], P('dp'), may hold values from 0 to 31999
- lengths: int32 [32], P('dp'), may hold values from 1 to 512, 9216 in all
- groups: int32 [32, 1], P('dp'), may hold values from 0 to 3
- baseline: float32 [4], replicated, may hold values from -2 to 0
Outputs:
- logprob: float32 [32, 512], P('dp')
- entropy: float32 [32, 512], P('dp')
- group_shift: float32 [2, 4], replicated
Inputs may be any that keep to these rules, and one draw needn't show every extreme that they name: `groups`: every group holds at least one sequence.
All inputs are finite; a program needn't handle non-finite values. No bound on the sum of `lengths` on one device may be relied on, other than what follows from the above.
Results may differ from a plain program's by a relative error of at most 0.00045.
The roundings to bfloat16 on the way count: a program that leaves them out, or rounds other values in their place, can miss the bound.
Values may be sent and summed in bfloat16 or wider, within the bound.
No kernel may reach another device: no remote copies, remote signals or barrier semaphores. Data moves between devices by JAX's collectives and lax.ppermute only.
A program may use at most 64 MiB of HBM per device.

v0:
```python
import jax
import jax.numpy as jnp
from jax import lax
from jax.sharding import PartitionSpec as P


def per_device(hidden, norm_gain, head, targets, lengths, groups, baseline):
    seq_count, slot_count, width = hidden.shape
    total_rows = seq_count * slot_count
    block = min(512, total_rows)
    weights = lax.all_gather(head, "dp", axis=0, tiled=True)
    vocab_width = weights.shape[1]
    offset = lax.axis_index("vocab") * vocab_width
    flat = hidden.reshape(total_rows, width).astype(jnp.float32)
    square = jnp.mean(flat * flat, axis=-1, keepdims=True)
    normed = (flat * lax.rsqrt(square + 1e-05) * norm_gain[None, :]).astype(jnp.bfloat16)
    positions = jnp.arange(slot_count, dtype=jnp.int32)
    live = (positions[None, :] < lengths[:, None]).reshape(total_rows)
    wanted = targets.reshape(total_rows)
    column = jnp.arange(vocab_width, dtype=jnp.int32) + offset

    def score(rows, picks):
        logits = jnp.dot(rows, weights, preferred_element_type=jnp.float32)
        local_top = jnp.max(logits, axis=-1)
        shifted = logits - local_top[:, None]
        expo = jnp.exp(shifted)
        local_total = jnp.sum(expo, axis=-1)
        local_spread = jnp.sum(expo * shifted, axis=-1)
        chosen = jnp.sum(jnp.where(column[None, :] == picks[:, None], logits, 0.0), axis=-1)
        top = lax.pmax(local_top, "vocab")
        factor = jnp.exp(local_top - top)
        total, spread, target = lax.psum(
            (
                local_total * factor,
                factor * (local_spread + local_total * (local_top - top)),
                chosen,
            ),
            "vocab",
        )
        return (target - top - jnp.log(total), jnp.log(total) - spread / total)

    blocks = (total_rows + block - 1) // block

    def advance(index, carry):
        out_lp, out_ent = carry
        start = index * block
        part_rows = lax.dynamic_slice_in_dim(normed, start, block, 0)
        part_picks = lax.dynamic_slice_in_dim(wanted, start, block, 0)
        block_lp, block_ent = score(part_rows, part_picks)
        out_lp = lax.dynamic_update_slice_in_dim(out_lp, block_lp, start, 0)
        out_ent = lax.dynamic_update_slice_in_dim(out_ent, block_ent, start, 0)
        return (out_lp, out_ent)

    empty = jnp.zeros((normed.shape[0],), jnp.float32)
    logprob, entropy = lax.fori_loop(0, blocks, advance, (empty, empty))
    logprob = jnp.where(live, logprob, 0.0).reshape(seq_count, slot_count)
    entropy = jnp.where(live, entropy, 0.0).reshape(seq_count, slot_count)
    group_count = baseline.shape[0]
    member = (groups[:, 0][:, None] == jnp.arange(group_count, dtype=jnp.int32)[None, :]).astype(
        jnp.float32
    )
    seq_sums = jnp.stack(
        [jnp.sum(logprob, axis=1), jnp.sum(entropy, axis=1), lengths.astype(jnp.float32)], axis=1
    )
    partial_value = jnp.dot(member.T, seq_sums, precision=lax.Precision.HIGHEST)
    group_lp, group_ent, group_cnt = lax.psum(
        (partial_value[:, 0], partial_value[:, 1], partial_value[:, 2]), "dp"
    )
    shift = jnp.stack([group_lp / group_cnt - baseline, group_ent / group_cnt], axis=0)
    return (logprob, entropy, shift)


def solution(mesh):
    placed = (
        P("dp", None, None),
        P(),
        P("dp", "vocab"),
        P("dp", None),
        P("dp"),
        P("dp", None),
        P(),
    )
    return jax.shard_map(
        per_device,
        mesh=mesh,
        in_specs=placed,
        out_specs=(P("dp", None), P("dp", None), P()),
        check_vma=False,
    )
```

profile of v0, /device:TPU:0, one launch (start us, length us, event | category | flops | bytes accessed | tf_op | source)
XLA Modules:
  0.0 203.4 jit_solution(1171368510043875422)
XLA Ops:
  7.2 0.0 all-gather.2.cloned.1.call-start
  7.2 0.7 all-gather.2.cloned.1.call-update
  7.9 2.1 %multiply_reduce_fusion = f32[2,512]{1,0:T(2,128)S(1)} fusion(bf16[2,512,1024]{2,1,0:T(8,128)(2,1)} %param.9), kind=kLoop, calls=%fused_computation.16 | loop fusion | flops 3144704 | bytes 2101248 | tf_op jit(solution)/shard_map/reduce_sum | solution.py:15
  10.0 0.7 copy.10
  10.7 0.7 iota_compare_fusion
  11.4 0.7 convert_bitcast_fusion
  12.1 2.1 %fusion.7 = bf16[1024,1024]{1,0:T(8,128)(2,1)S(1)} fusion(f32[1024]{0:T(1024)} %param.10, f32[1024]{0:T(1024)S(1)} %bitcast.30, bf16[2,512,1024]{2,1,0:T(8,128)(2,1)} %param.9), kind=kLoop, calls=%fused_computation.15 | loop fusion | flops 4194304 | bytes 4202496 | tf_op jit(solution)/shard_map/convert_element_type | solution.py:16
  14.3 69.3 %all-gather.2.cloned.1.call-done = bf16[1024,4000]{1,0:T(8,128)(2,1)} async-done(((bf16[64,4000]{1,0:T(8,128)(2,1)}), bf16[1024,4000]{1,0:T(8,128)(2,1)}) %all-gather.2.cloned.1.call-update) | async-done | bytes 8192016 | tf_op jit(solution)/shard_map/all_gather | solution.py:11
  83.6 0.0 copy-start.3
  83.6 0.0 copy-start.2
  83.6 73.4 %while.16 = (s32[]{:T(128)}, f32[1024]{0:T(1024)S(1)}, f32[1024]{0:T(1024)S(1)}, s32[1024]{0:T(1024)S(1)}, bf16[1024,1024]{1,0:T(8,128)(2,1)S(1)}, /*index=5*/bf...) while((s32[]{:T(128)}, f32[1024]{0:T(1024)S(1)}, ...), condition=%wide.region_10.11_spmd.clone, body=%wide.region_1.10_spmd.clone.sunk | while | flops 4210696704 | bytes 25714092 | solution.py:55
  83.6 7.1 %fusion.24 = (f32[512]{0:T(512)S(1)}, f32[512,4000]{0,1:T(8,128)S(1)}) fusion(bf16[1024,4000]{1,0:T(8,128)(2,1)} %get-tuple-element.277, bf16[1024,1024]{1,0:T(8,128)(2,1)S(1)} %get-tuple-element.276, s32[]{:T(128)S(6)} %select_n.33), kind=kOutput, calls=%fused_computation.38.clone.1 | convolution fusion | flops 4196351488 | bytes 17434628 | tf_op jit(solution)/shard_map/while/body/eval_jaxpr/dot_general | solution.py:23
  90.7 0.1 dynamic_slice.23
  90.8 3.2 %fusion.25 = (f32[512]{0:T(512)S(1)}, f32[512]{0:T(512)S(1)}, f32[512]{0:T(512)S(1)}) fusion(f32[512,4000]{0,1:T(8,128)S(1)} %get-tuple-element.238, f32[512]{0:T(512)S(1)} %get-tuple-element.239, s32[512]{0:T(512)S(1)} %dynamic_slice.23, s32[4000]{0:T(1024)S(1)} %iota_add_fusion.2), kind=kLoop, calls=%fused_computation.3.clone.1 | loop fusion | flops 14334464 | bytes 8218240 | tf_op jit(solution)/shard_map/while/body/eval_jaxpr/reduce_sum | solution.py:28
  94.1 14.4 %pmax.13 = f32[512]{0:T(512)S(1)} all-reduce(f32[512]{0:T(512)S(1)} %get-tuple-element.239), channel_id=1, replica_groups=mesh['dp'=16,'vocab'=8] {'vocab'}, use_global_device_ids=true, to_apply=%region_5.5 | all-reduce | flops 512 | bytes 4096 | tf_op jit(solution)/shard_map/while/body/eval_jaxpr/pmax | solution.py:30
  108.5 12.6 %all-reduce.3 = (f32[512]{0:T(512)S(1)}, f32[512]{0:T(512)S(1)}, f32[512]{0:T(512)S(1)}) all-reduce(f32[512]{0:T(512)S(1)} %get-tuple-element.240, f32[512]{0:T(512)S(1)} %get-tuple-element.243, f32[512]{0:T(512)S(1)} %get-tuple-element.244), channel_id=1, replica_groups=mesh['dp'=16,'vocab'=8] {'vocab'}, use_global_device_ids=true, to_apply=%region_3.0 | all-reduce | flops 1536 | bytes 12288 | tf_op jit(solution)/shard_map/while/body/eval_jaxpr/psum | solution.py:32
  121.1 0.1 subtract_dynamic-update-slice_fusion.3
  121.3 7.1 %fusion.24 = (f32[512]{0:T(512)S(1)}, f32[512,4000]{0,1:T(8,128)S(1)}) fusion(bf16[1024,4000]{1,0:T(8,128)(2,1)} %get-tuple-element.277, bf16[1024,1024]{1,0:T(8,128)(2,1)S(1)} %get-tuple-element.276, s32[]{:T(128)S(6)} %select_n.33), kind=kOutput, calls=%fused_computation.38.clone.1 | convolution fusion | flops 4196351488 | bytes 17434628 | tf_op jit(solution)/shard_map/while/body/eval_jaxpr/dot_general | solution.py:23
  128.4 0.1 dynamic_slice.23
  128.5 3.2 %fusion.25 = (f32[512]{0:T(512)S(1)}, f32[512]{0:T(512)S(1)}, f32[512]{0:T(512)S(1)}) fusion(f32[512,4000]{0,1:T(8,128)S(1)} %get-tuple-element.238, f32[512]{0:T(512)S(1)} %get-tuple-element.239, s32[512]{0:T(512)S(1)} %dynamic_slice.23, s32[4000]{0:T(1024)S(1)} %iota_add_fusion.2), kind=kLoop, calls=%fused_computation.3.clone.1 | loop fusion | flops 14334464 | bytes 8218240 | tf_op jit(solution)/shard_map/while/body/eval_jaxpr/reduce_sum | solution.py:28
  131.7 12.4 %pmax.13 = f32[512]{0:T(512)S(1)} all-reduce(f32[512]{0:T(512)S(1)} %get-tuple-element.239), channel_id=1, replica_groups=mesh['dp'=16,'vocab'=8] {'vocab'}, use_global_device_ids=true, to_apply=%region_5.5 | all-reduce | flops 512 | bytes 4096 | tf_op jit(solution)/shard_map/while/body/eval_jaxpr/pmax | solution.py:30
  144.2 12.6 %all-reduce.3 = (f32[512]{0:T(512)S(1)}, f32[512]{0:T(512)S(1)}, f32[512]{0:T(512)S(1)}) all-reduce(f32[512]{0:T(512)S(1)} %get-tuple-element.240, f32[512]{0:T(512)S(1)} %get-tuple-element.243, f32[512]{0:T(512)S(1)} %get-tuple-element.244), channel_id=1, replica_groups=mesh['dp'=16,'vocab'=8] {'vocab'}, use_global_device_ids=true, to_apply=%region_3.0 | all-reduce | flops 1536 | bytes 12288 | tf_op jit(solution)/shard_map/while/body/eval_jaxpr/psum | solution.py:32
  156.8 0.1 subtract_dynamic-update-slice_fusion.3
  157.0 0.0 copy-start
  157.0 0.0 copy-start.1
  157.0 0.1 reduce_sum.67
  157.1 0.1 reduce_sum.68
  157.3 0.0 copy-done.3
  157.3 0.2 fusion.8
  157.5 38.5 %all-reduce.1 = (f32[4]{0:T(128)S(1)}, f32[4]{0:T(128)S(1)}, f32[4]{0:T(128)S(1)}) all-reduce(f32[4]{0:T(128)S(1)} %get-tuple-element.177, f32[4]{0:T(128)S(1)} %get-tuple-element.178, f32[4]{0:T(128)S(1)} %get-tuple-element.176), channel_id=1, replica_groups=mesh['dp'=16,'vocab'=8] {'dp'}, use_global_device_ids=true, to_apply=%region_15.16 | all-reduce | flops 12 | bytes 96 | tf_op jit(solution)/shard_map/psum | solution.py:66
  195.9 0.0 copy-done.2
  195.9 0.6 pad_maximum_fusion
  196.5 0.0 copy-done
  196.5 0.0 copy-done.1
  (14 shorter events, 0.1 us)
Async XLA Ops:
  7.2 76.4 %all-gather.2.cloned.1.call-start = ((), (), s32[]{:S(2)}) async-start(), calls=%async_computation | async-start | bytes 8912896 | tf_op jit(solution)/shard_map/all_gather | solution.py:11
  83.6 73.7 %copy-start.3 = (s32[2,1]{0,1:T(1,128)S(1)}, s32[2,1]{0,1:T(1,128)}, u32[]{:S(2)}) copy-start(s32[2,1]{0,1:T(1,128)} %param.14) | copy-start | bytes 28
  83.6 112.3 %copy-start.2 = (f32[4]{0:T(128)S(1)}, f32[4]{0:T(128)}, u32[]{:S(2)}) copy-start(f32[4]{0:T(128)} %param.15) | copy-start | bytes 52
  157.0 39.5 %copy-start = (f32[2,512]{1,0:T(2,128)}, f32[2,512]{1,0:T(2,128)S(1)}, u32[]{:S(2)}) copy-start(f32[2,512]{1,0:T(2,128)S(1)} %reshape.45) | copy-start | bytes 12292
  157.0 39.5 %copy-start.1 = (f32[2,512]{1,0:T(2,128)}, f32[2,512]{1,0:T(2,128)S(1)}, u32[]{:S(2)}) copy-start(f32[2,512]{1,0:T(2,128)S(1)} %reshape.46) | copy-start | bytes 12292
Sparse Core Ops, SparseCore 0:
  10.1 73.4 all-gather.1
where the time goes:
time: 204 us; the launch traced here: 203 us
  blocking collectives  90.5 us (44%)
  waiting for transfers between devices  70 us (34%)
  matrix products  14.4 us (7%)
  between operations  14.1 us (7%)
  other arithmetic  13.3 us (7%)
    all_gather x1, waiting for transfers between devices, per_device(): weights = lax.all_gather(head, 'dp', axis=0, tiled=True)  69.3 us
    psum x1, blocking collectives, per_device(): lax.psum((partial_value[:, 0], partial_value[:, 1], partial_value[:, 2]),...  38.5 us
    pmax x2, blocking collectives, score(): top = lax.pmax(local_top, 'vocab')  26.8 us
    psum x2, blocking collectives, score(): lax.psum((local_total * factor, factor * (local_spread + local_total * (l...  25.3 us
    dot_general x2, matrix products, score(): logits = jnp.dot(rows, weights, preferred_element_type=jnp.float32)  14.3 us
    reduce_sum x2, other arithmetic, score(): local_spread = jnp.sum(expo * shifted, axis=-1)  6.5 us
  transfers between devices with their start and end apart: 1, of which 1 were waited for; matrix products, arithmetic and copies ran while one was open for 3% of the time, Pallas kernels for 0%

commit v1 on v0

--- a/solution.py
+++ b/solution.py
@@ -8,7 +8,12 @@
     seq_count, slot_count, width = hidden.shape
     total_rows = seq_count * slot_count
     block = min(512, total_rows)
-    weights = lax.all_gather(head, "dp", axis=0, tiled=True)
+    weights = jnp.concatenate(
+        lax.all_to_all(
+            jnp.stack(lax.axis_size("dp") * [head]), axis_name="dp", split_axis=0, concat_axis=0
+        ),
+        axis=0,
+    )
     vocab_width = weights.shape[1]
     offset = lax.axis_index("vocab") * vocab_width
     flat = hidden.reshape(total_rows, width).astype(jnp.float32)

time: 204 us -> 250 us (1.23)
  waiting for transfers between devices: 70 us -> 122 us
  between operations: 14.1 us -> 0.74 us
  starting transfers between devices: 0.04 us -> 8.35 us
  local copies, waits for them, and re-layouts: 0.92 us -> 5.57 us
  other arithmetic: 13.3 us -> 10.1 us
    all_to_all x0 -> x1, waiting for transfers between devices: none -> 122 us  [per_device(): lax.all_to_all(jnp.stack(lax.axis_size('dp') * [head]), axis_name='dp', s...]
    all_gather x1 -> x0, waiting for transfers between devices: 69.3 us -> none  [per_device(): weights = lax.all_gather(head, 'dp', axis=0, tiled=True)]
    all_to_all x0 -> x1, starting transfers between devices: none -> 8.35 us  [per_device(): lax.all_to_all(jnp.stack(lax.axis_size('dp') * [head]), axis_name='dp', s...]
    another operation x0 -> x1, local copies, waits for them, and re-layouts: none -> 5.33 us  [per_device(): jnp.stack(lax.axis_size('dp') * [head])]
  transfers between devices with their start and end apart: 1 -> 1, of which waited for: 1 -> 1; matrix products, arithmetic and copies ran while one was open for 3% -> 1% of each run, Pallas kernels for 0% -> 0%
where the time goes in v1:
time: 250 us
  waiting for transfers between devices  122 us (49%)
  blocking collectives  88.5 us (35%)
  matrix products  15.1 us (6%)
  other arithmetic  10.1 us (4%)
  starting transfers between devices  8.35 us (3%)
  local copies, waits for them, and re-layouts  5.57 us (2%)
    all_to_all x1, waiting for transfers between devices, per_device(): lax.all_to_all(jnp.stack(lax.axis_size('dp') * [head]), axis_name='dp', s...  122 us
    psum x1, blocking collectives, per_device(): lax.psum((partial_value[:, 0], partial_value[:, 1], partial_value[:, 2]),...  37.3 us
    pmax x2, blocking collectives, score(): top = lax.pmax(local_top, 'vocab')  25.9 us
    psum x2, blocking collectives, score(): lax.psum((local_total * factor, factor * (local_spread + local_total * (l...  25.3 us
    dot_general x2, matrix products, score(): logits = jnp.dot(rows, weights, preferred_element_type=jnp.float32)  14.9 us
    all_to_all x1, starting transfers between devices, per_device(): lax.all_to_all(jnp.stack(lax.axis_size('dp') * [head]), axis_name='dp', s...  8.35 us
    reduce_sum x2, other arithmetic, score(): local_spread = jnp.sum(expo * shifted, axis=-1)  6.47 us
    another operation x1, local copies, waits for them, and re-layouts, per_device(): jnp.stack(lax.axis_size('dp') * [head])  5.33 us
  transfers between devices with their start and end apart: 1, of which 1 were waited for; matrix products, arithmetic and copies ran while one was open for 1% of the time, Pallas kernels for 0%

profile of v1, /device:TPU:0, one launch (start us, length us, event | category | flops | bytes accessed | tf_op | source)
XLA Modules:
  0.0 250.1 jit_solution(11141085017558665829)
XLA Ops:
  0.6 5.3 %stack.16 = bf16[16,64,4000]{2,1,0:T(8,128)(2,1)} broadcast(bf16[64,4000]{1,0:T(8,128)(2,1)} %param.11), dimensions={1,2} | broadcast | bytes 8704000 | tf_op jit(solution)/shard_map/stack | solution.py:13
  6.0 0.0 copy-start
  6.0 0.0 copy-start.3
  6.0 0.0 copy-start.5
  6.0 0.0 copy-start.4
  6.0 8.4 %all-to-all-start = ((bf16[16,64,4000]{2,1,0:T(8,128)(2,1)}), bf16[16,64,4000]{2,1,0:T(8,128)(2,1)}, u32[]{:S(2)}, u32[]{:S(2)}) async-start(bf16[16,64,4000]{2,1,0:T(8,128)(2,1)} %stack.16), calls=%async_computation | async-start | bytes 16777216 | tf_op jit(solution)/shard_map/all_to_all | solution.py:12
  14.3 0.0 copy-done
  14.3 0.5 multiply_reduce_fusion
  14.9 0.0 copy-done.3
  14.9 0.0 copy-done.5
  14.9 0.1 iota_compare_fusion
  15.0 0.0 copy-done.4
  15.0 1.9 fusion.7
  16.9 121.6 %all-to-all-done = bf16[16,64,4000]{2,1,0:T(8,128)(2,1)} async-done(((bf16[16,64,4000]{2,1,0:T(8,128)(2,1)}), bf16[16,64,4000]{2,1,0:T(8,128)(2,1)}, u32[]{:S(2)}, u32[]{:S(2)}) %all-to-all-start) | async-done | bytes 8192032 | tf_op jit(solution)/shard_map/all_to_all | solution.py:12
  138.5 0.0 copy-start.7
  138.5 0.0 copy-start.6
  138.5 73.1 %while.16 = (s32[]{:T(128)}, f32[1024]{0:T(1024)S(1)}, f32[1024]{0:T(1024)S(1)}, s32[1024]{0:T(1024)S(1)}, bf16[1024,1024]{1,0:T(8,128)(2,1)}, /*index=5*/bf16[1...) while((s32[]{:T(128)}, f32[1024]{0:T(1024)S(1)}, ...), condition=%wide.region_10.11_spmd.clone, body=%wide.region_1.10_spmd.clone.sunk | while | flops 4210696704 | bytes 25910700 | solution.py:60
  138.5 7.5 %fusion.24 = (f32[512]{0:T(512)S(1)}, f32[512,4000]{0,1:T(8,128)S(1)}) fusion(bf16[1024,4000]{1,0:T(8,128)(2,1)} %get-tuple-element.277, bf16[1024,1024]{1,0:T(8,128)(2,1)} %get-tuple-element.276, s32[]{:T(128)S(6)} %select_n.33), kind=kOutput, calls=%fused_computation.38.clone.1 | convolution fusion | flops 4196351488 | bytes 17631236 | tf_op jit(solution)/shard_map/while/body/eval_jaxpr/dot_general | solution.py:28
  146.0 0.1 dynamic_slice.23
  146.1 3.2 %fusion.25 = (f32[512]{0:T(512)S(1)}, f32[512]{0:T(512)S(1)}, f32[512]{0:T(512)S(1)}) fusion(f32[512,4000]{0,1:T(8,128)S(1)} %get-tuple-element.238, f32[512]{0:T(512)S(1)} %get-tuple-element.239, s32[512]{0:T(512)S(1)} %dynamic_slice.23, s32[4000]{0:T(1024)S(1)} %iota_add_fusion.2), kind=kLoop, calls=%fused_computation.3.clone.1 | loop fusion | flops 14334464 | bytes 8218240 | tf_op jit(solution)/shard_map/while/body/eval_jaxpr/reduce_sum | solution.py:33
  149.3 13.5 %pmax.13 = f32[512]{0:T(512)S(1)} all-reduce(f32[512]{0:T(512)S(1)} %get-tuple-element.239), channel_id=1, replica_groups=mesh['dp'=16,'vocab'=8] {'vocab'}, use_global_device_ids=true, to_apply=%region_5.5 | all-reduce | flops 512 | bytes 4096 | tf_op jit(solution)/shard_map/while/body/eval_jaxpr/pmax | solution.py:35
  162.8 12.6 %all-reduce.3 = (f32[512]{0:T(512)S(1)}, f32[512]{0:T(512)S(1)}, f32[512]{0:T(512)S(1)}) all-reduce(f32[512]{0:T(512)S(1)} %get-tuple-element.240, f32[512]{0:T(512)S(1)} %get-tuple-element.243, f32[512]{0:T(512)S(1)} %get-tuple-element.244), channel_id=1, replica_groups=mesh['dp'=16,'vocab'=8] {'vocab'}, use_global_device_ids=true, to_apply=%region_3.0 | all-reduce | flops 1536 | bytes 12288 | tf_op jit(solution)/shard_map/while/body/eval_jaxpr/psum | solution.py:37
  175.5 0.1 subtract_dynamic-update-slice_fusion.3
  175.6 7.5 %fusion.24 = (f32[512]{0:T(512)S(1)}, f32[512,4000]{0,1:T(8,128)S(1)}) fusion(bf16[1024,4000]{1,0:T(8,128)(2,1)} %get-tuple-element.277, bf16[1024,1024]{1,0:T(8,128)(2,1)} %get-tuple-element.276, s32[]{:T(128)S(6)} %select_n.33), kind=kOutput, calls=%fused_computation.38.clone.1 | convolution fusion | flops 4196351488 | bytes 17631236 | tf_op jit(solution)/shard_map/while/body/eval_jaxpr/dot_general | solution.py:28
  183.1 0.1 dynamic_slice.23
  183.2 3.2 %fusion.25 = (f32[512]{0:T(512)S(1)}, f32[512]{0:T(512)S(1)}, f32[512]{0:T(512)S(1)}) fusion(f32[512,4000]{0,1:T(8,128)S(1)} %get-tuple-element.238, f32[512]{0:T(512)S(1)} %get-tuple-element.239, s32[512]{0:T(512)S(1)} %dynamic_slice.23, s32[4000]{0:T(1024)S(1)} %iota_add_fusion.2), kind=kLoop, calls=%fused_computation.3.clone.1 | loop fusion | flops 14334464 | bytes 8218240 | tf_op jit(solution)/shard_map/while/body/eval_jaxpr/reduce_sum | solution.py:33
  186.4 12.4 %pmax.13 = f32[512]{0:T(512)S(1)} all-reduce(f32[512]{0:T(512)S(1)} %get-tuple-element.239), channel_id=1, replica_groups=mesh['dp'=16,'vocab'=8] {'vocab'}, use_global_device_ids=true, to_apply=%region_5.5 | all-reduce | flops 512 | bytes 4096 | tf_op jit(solution)/shard_map/while/body/eval_jaxpr/pmax | solution.py:35
  198.8 12.6 %all-reduce.3 = (f32[512]{0:T(512)S(1)}, f32[512]{0:T(512)S(1)}, f32[512]{0:T(512)S(1)}) all-reduce(f32[512]{0:T(512)S(1)} %get-tuple-element.240, f32[512]{0:T(512)S(1)} %get-tuple-element.243, f32[512]{0:T(512)S(1)} %get-tuple-element.244), channel_id=1, replica_groups=mesh['dp'=16,'vocab'=8] {'vocab'}, use_global_device_ids=true, to_apply=%region_3.0 | all-reduce | flops 1536 | bytes 12288 | tf_op jit(solution)/shard_map/while/body/eval_jaxpr/psum | solution.py:37
  211.5 0.1 subtract_dynamic-update-slice_fusion.3
  211.7 0.0 copy-start.1
  211.7 0.0 copy-start.2
  211.7 0.1 reduce_sum.67
  211.8 0.1 reduce_sum.68
  211.9 0.0 copy-done.7
  211.9 0.2 fusion.8
  212.1 37.3 %all-reduce.1 = (f32[4]{0:T(128)S(1)}, f32[4]{0:T(128)S(1)}, f32[4]{0:T(128)S(1)}) all-reduce(f32[4]{0:T(128)S(1)} %get-tuple-element.177, f32[4]{0:T(128)S(1)} %get-tuple-element.178, f32[4]{0:T(128)S(1)} %get-tuple-element.176), channel_id=1, replica_groups=mesh['dp'=16,'vocab'=8] {'dp'}, use_global_device_ids=true, to_apply=%region_15.16 | all-reduce | flops 12 | bytes 96 | tf_op jit(solution)/shard_map/psum | solution.py:71
  249.5 0.0 copy-done.6
  249.5 0.6 pad_maximum_fusion
  250.0 0.0 copy-done.1
  250.1 0.0 copy-done.2
  (16 shorter events, 0.1 us)
Async XLA Ops:
  6.0 8.4 %copy-start = (bf16[2,512,1024]{2,1,0:T(8,128)(2,1)S(1)}, bf16[2,512,1024]{2,1,0:T(8,128)(2,1)}, u32[]{:S(2)}) copy-start(bf16[2,512,1024]{2,1,0:T(8,128)(2,1)} %param.9) | copy-start | bytes 6291460
  6.0 8.9 %copy-start.3 = (s32[2,512]{1,0:T(2,128)S(1)}, s32[2,512]{1,0:T(2,128)}, u32[]{:S(2)}) copy-start(s32[2,512]{1,0:T(2,128)} %param.12) | copy-start | bytes 12292
  6.0 8.9 %copy-start.5 = (s32[2]{0:T(128)S(1)}, s32[2]{0:T(128)}, u32[]{:S(2)}) copy-start(s32[2]{0:T(128)} %param.13) | copy-start | bytes 28
  6.0 9.0 %copy-start.4 = (f32[1024]{0:T(1024)S(1)}, f32[1024]{0:T(1024)}, u32[]{:S(2)}) copy-start(f32[1024]{0:T(1024)} %param.10) | copy-start | bytes 12292
  6.0 132.5 %all-to-all-start = ((bf16[16,64,4000]{2,1,0:T(8,128)(2,1)}), bf16[16,64,4000]{2,1,0:T(8,128)(2,1)}, u32[]{:S(2)}, u32[]{:S(2)}) async-start(bf16[16,64,4000]{2,1,0:T(8,128)(2,1)} %stack.16), calls=%async_computation | async-start | bytes 16777216 | tf_op jit(solution)/shard_map/all_to_all | solution.py:12
  138.5 73.5 %copy-start.7 = (s32[2,1]{0,1:T(1,128)S(1)}, s32[2,1]{0,1:T(1,128)}, u32[]{:S(2)}) copy-start(s32[2,1]{0,1:T(1,128)} %param.14) | copy-start | bytes 28
  138.5 111.0 %copy-start.6 = (f32[4]{0:T(128)S(1)}, f32[4]{0:T(128)}, u32[]{:S(2)}) copy-start(f32[4]{0:T(128)} %param.15) | copy-start | bytes 52
  211.7 38.4 %copy-start.1 = (f32[2,512]{1,0:T(2,128)}, f32[2,512]{1,0:T(2,128)S(1)}, u32[]{:S(2)}) copy-start(f32[2,512]{1,0:T(2,128)S(1)} %reshape.51) | copy-start | bytes 12292
  211.7 38.4 %copy-start.2 = (f32[2,512]{1,0:T(2,128)}, f32[2,512]{1,0:T(2,128)S(1)}, u32[]{:S(2)}) copy-start(f32[2,512]{1,0:T(2,128)S(1)} %reshape.52) | copy-start | bytes 12292
